TPU v7x, 128 devices: a whole 4x4x4 slice. The times are simulated.
128 devices in a mesh: expert: 32 (over x_lo, z, y), replica: 4 (over x_hi, core).
Axes of the slice: x: 4 (x_hi: 2, x_lo: 2; x = x_hi * 2 + x_lo), y: 4, z: 4, core: 2. Of those that a mesh axis runs over, the one named last changes fastest.
Arguments:
- tokens: bfloat16 [32768, 7168], P(('expert', 'replica')), may hold values from -6 to 6
- routes: int32 [32768, 8], P(('expert', 'replica')), may hold values from 0 to 255, all different within a row
- counts: int32 [128], P(('expert', 'replica')), may hold values from 128 to 256, as said below
- w_gate: bfloat16 [32, 7168, 2048], P('expert', None, 'replica'), may hold values from -0.0625 to 0.0625
- w_up: bfloat16 [32, 7168, 2048], P('expert', None, 'replica'), may hold values from -0.0625 to 0.0625
Outputs:
- key_cov: float32 [32, 2048, 2048], P('expert', 'replica')
Inputs may be any that keep to these rules, and one draw needn't show every extreme that they name: `counts`: every count is a multiple of 128; some device has 256 and some 128.
All inputs are finite; a program needn't handle non-finite values.
Results may differ from a plain program's by a relative error of at most 0.0039.
Values may be sent and summed in bfloat16 or wider, within the bound.
No kernel may reach another device: no remote copies, remote signals or barrier semaphores. Data moves between devices by JAX's collectives and lax.ppermute only.
A program may use at most 128 MiB of HBM per device.

v0:
```python
import jax
import jax.numpy as jnp
from jax import lax
from jax.sharding import Mesh, NamedSharding, PartitionSpec as P

N_ROUTED = 256
TOP = 8


def slot_onehot(routes, real_count, expert_total, capacity):
    tokens_here = routes.shape[0]
    token = lax.broadcasted_iota(jnp.int32, (tokens_here, 1), 0)
    expert = lax.broadcasted_iota(jnp.int32, (1, 1, expert_total), 2)
    hit = jnp.any(routes[:, :, None] == expert, axis=1) & (token < real_count)
    row = lax.broadcasted_iota(jnp.int32, (tokens_here, tokens_here), 0)
    col = lax.broadcasted_iota(jnp.int32, (tokens_here, tokens_here), 1)
    earlier = (col < row).astype(jnp.bfloat16)
    rank = jnp.dot(earlier, hit.astype(jnp.bfloat16), preferred_element_type=jnp.float32)
    rank = rank.astype(jnp.int32)
    slot = lax.broadcasted_iota(jnp.int32, (1, capacity, 1), 1)
    return hit.T[:, None, :] & (rank.T[:, None, :] == slot)


def body(tokens, routes, counts, w_gate, w_up):
    expert_count = lax.axis_size("expert")
    half_count = lax.axis_size("xh")
    core_count = lax.axis_size("core")
    slot_total, width_model = tokens.shape
    capacity = slot_total * TOP // N_ROUTED
    onehot = slot_onehot(routes, counts[0], expert_count, capacity)
    onehot = jnp.broadcast_to(
        onehot[:, None], (expert_count, half_count, capacity, slot_total)
    ).reshape(expert_count * half_count * capacity, slot_total)
    slot_rows = jnp.dot(
        onehot.astype(tokens.dtype), tokens, preferred_element_type=jnp.float32
    ).astype(tokens.dtype)
    slot_rows = slot_rows.reshape(expert_count * half_count, capacity, width_model)
    slot_block = lax.all_to_all(
        slot_rows, ("expert", "xh"), split_axis=0, concat_axis=0, tiled=True
    )
    slot_block = slot_block.reshape(expert_count * half_count * capacity, width_model)
    slot_block = lax.all_gather(slot_block, "core", axis=0, tiled=True)
    gate_pre = jnp.dot(slot_block, w_gate[0], preferred_element_type=jnp.float32)
    up_pre = jnp.dot(slot_block, w_up[0], preferred_element_type=jnp.float32)
    own_keys = (jax.nn.silu(gate_pre) * up_pre).astype(jnp.bfloat16)
    factor = 1.0 / (expert_count * capacity)
    key_gram = (
        jnp.einsum(
            "rf,rg->fg",
            own_keys,
            lax.all_gather(own_keys, ("xh", "core"), axis=1, tiled=True),
            preferred_element_type=jnp.float32,
        )
        * factor
    )
    return key_gram[None]


def solution(mesh):
    expert_count, replica_count = mesh.devices.shape
    split = Mesh(
        mesh.devices.reshape(expert_count, 2, replica_count // 2), ("expert", "xh", "core")
    )
    rows = ("expert", "xh", "core")
    step = jax.shard_map(
        body,
        mesh=split,
        in_specs=(
            P(rows, None),
            P(rows, None),
            P(rows),
            P("expert", None, ("xh", "core")),
            P("expert", None, ("xh", "core")),
        ),
        out_specs=P("expert", ("xh", "core"), None),
        check_vma=False,
    )
    out_sharding = NamedSharding(mesh, P("expert", "replica", None))

    def run(tokens, routes, counts, w_gate, w_up):
        out = step(tokens, routes, counts, w_gate, w_up)
        return lax.with_sharding_constraint(out, out_sharding)

    return run
```

profile of v0, /device:TPU:1, one launch (start us, length us, event | category | flops | bytes accessed | tf_op | source)
XLA Modules:
  0.0 215.0 jit_solution(5587718582403345066)
XLA Ops:
  6.5 0.0 all-gather.3.cloned.1.call-start
  7.2 0.7 fusion.7
  8.0 0.2 convolution_convert_fusion.1
  8.1 0.1 fusion.8
  8.3 4.1 %fusion = bf16[64,8,7168]{2,1,0:T(8,128)(2,1)S(1)} fusion(pred[512,256]{1,0:T(8,128)(4,1)S(1)} %bitcast.25, bf16[256,7168]{1,0:T(8,128)(2,1)} %param.5), kind=kOutput, calls=%fused_computation.1 | convolution fusion | flops 1882718208 | bytes 11141120 | tf_op jit(solution)/shard_map/dot_general | solution.py:34
  12.4 96.3 %all_to_all.5 = bf16[64,8,7168]{2,1,0:T(8,128)(2,1)} all-to-all(bf16[64,8,7168]{2,1,0:T(8,128)(2,1)S(1)} %fusion), channel_id=1, replica_groups=mesh['expert'=32,'xh'=2,'core'=2] {'expert','xh'}, dimensions={0} | all-to-all | bytes 14680064 | tf_op jit(solution)/shard_map/all_to_all | solution.py:38
  108.7 0.0 all-gather.3.cloned.1.call-update
  108.7 0.0 all-gather.5.cloned.1.call-start
  108.8 28.3 %all-gather.3.cloned.1.call-done = bf16[1024,7168]{1,0:T(8,128)(2,1)} async-done(((bf16[512,7168]{1,0:T(8,128)(2,1)}), bf16[1024,7168]{1,0:T(8,128)(2,1)}) %all-gather.3.cloned.1.call-update) | async-done | bytes 14680080 | tf_op jit(solution)/shard_map/all_gather | solution.py:42
  137.1 0.0 copy-start
  137.1 13.3 %fusion.1 = f32[1024,512]{1,0:T(8,128)S(1)} fusion(bf16[1024,7168]{1,0:T(8,128)(2,1)} %all-gather.3.cloned.1.call-done, bf16[1,7168,512]{2,1,0:T(8,128)(2,1)} %param.9), kind=kOutput, calls=%fused_computation.2 | convolution fusion | flops 7516192768 | bytes 24117248 | tf_op jit(solution)/shard_map/dot_general | solution.py:44
  150.4 0.0 copy-done
  150.4 10.8 %multiply_convert_fusion = bf16[1024,512]{1,0:T(8,128)(2,1)} fusion(f32[1024,512]{1,0:T(8,128)S(1)} %fusion.1, bf16[1024,7168]{1,0:T(8,128)(2,1)S(1)} %copy-done, bf16[1,7168,512]{2,1,0:T(8,128)(2,1)} %param.8), kind=kOutput, calls=%fused_computation.7 | convolution fusion | flops 7519338496 | bytes 25165824 | tf_op jit(solution)/shard_map/dot_general | solution.py:43
  161.3 0.0 all-gather.5.cloned.1.call-update
  161.3 39.9 %all-gather.5.cloned.1.call-done = bf16[1024,2048]{1,0:T(8,128)(2,1)} async-done(((bf16[1024,512]{1,0:T(8,128)(2,1)}), bf16[1024,2048]{1,0:T(8,128)(2,1)}) %all-gather.5.cloned.1.call-update) | async-done | bytes 4194320 | tf_op jit(solution)/shard_map/all_gather | solution.py:51
  201.2 6.9 %multiply_bitcast_fusion = f32[1,512,2048]{2,1,0:T(8,128)} fusion(bf16[1024,512]{1,0:T(8,128)(2,1)} %multiply_convert_fusion, bf16[1024,2048]{1,0:T(8,128)(2,1)} %all-gather.5.cloned.1.call-done), kind=kOutput, calls=%fused_computation.6 | convolution fusion | flops 2148532224 | bytes 9437184 | tf_op jit(solution)/shard_map/rf,rg->fg/dot_general | solution.py:48
  (3 shorter events, 0.1 us)
Async XLA Ops:
  6.5 130.6 %all-gather.3.cloned.1.call-start = ((), (), s32[]{:S(2)}) async-start(), calls=%async_computation.1 | async-start | bytes 22020096 | tf_op jit(solution)/shard_map/all_gather | solution.py:42
  108.7 92.5 %all-gather.5.cloned.1.call-start = ((), (), s32[]{:S(2)}) async-start(), calls=%async_computation.2 | async-start | bytes 5242880 | tf_op jit(solution)/shard_map/all_gather | solution.py:51
  137.1 13.3 %copy-start = (bf16[1024,7168]{1,0:T(8,128)(2,1)S(1)}, bf16[1024,7168]{1,0:T(8,128)(2,1)}, u32[]{:S(2)}) copy-start(bf16[1024,7168]{1,0:T(8,128)(2,1)} %all-gather.3.cloned.1.call-done) | copy-start | bytes 44040196
Sparse Core Ops, SparseCore 0:
  108.9 28.2 all-gather.2
  161.4 39.7 all-gather.4
where the time goes:
time: 215 us
  blocking collectives  96.3 us (45%)
  waiting for transfers between devices  68.3 us (32%)
  matrix products  35.3 us (16%)
  between operations  14.1 us (7%)
    all_to_all x1, blocking collectives, body(): lax.all_to_all(slot_rows, ('expert', 'xh'), split_axis=0, concat_axis=0,...  96.3 us
    all_gather x1, waiting for transfers between devices, body(): lax.all_gather(own_keys, ('xh', 'core'), axis=1, tiled=True)  39.9 us
    all_gather x1, waiting for transfers between devices, body(): slot_block = lax.all_gather(slot_block, 'core', axis=0, tiled=True)  28.3 us
    dot_general x1, matrix products, body(): up_pre = jnp.dot(slot_block, w_up[0], preferred_element_type=jnp.float32)  13.3 us
    dot_general x1, matrix products, body(): jnp.dot(slot_block, w_gate[0], preferred_element_type=jnp.float32)  10.8 us
    dot_general x1, matrix products, body(): jnp.einsum('rf,rg->fg', own_keys, lax.all_gather(own_keys, ('xh', 'core')...  6.9 us
  transfers between devices with their start and end apart: 2, of which 2 were waited for; matrix products, arithmetic and copies ran while one was open for 0% of the time, Pallas kernels for 0%

commit v1 on v0

--- a/solution.py
+++ b/solution.py
@@ -39,7 +39,9 @@
         slot_rows, ("expert", "xh"), split_axis=0, concat_axis=0, tiled=True
     )
     slot_block = slot_block.reshape(expert_count * half_count * capacity, width_model)
-    slot_block = lax.all_gather(slot_block, "core", axis=0, tiled=True)
+    slot_block = jnp.concatenate(
+        lax.all_to_all(jnp.stack([slot_block] * lax.axis_size("core")), "core", 0, 0), axis=0
+    )
     gate_pre = jnp.dot(slot_block, w_gate[0], preferred_element_type=jnp.float32)
     up_pre = jnp.dot(slot_block, w_up[0], preferred_element_type=jnp.float32)
     own_keys = (jax.nn.silu(gate_pre) * up_pre).astype(jnp.bfloat16)

time: 215 us -> 195 us (0.907)
  waiting for transfers between devices: 68.3 us -> 34.9 us
  blocking collectives: 96.3 us -> 114 us
  matrix products: 35.3 us -> 29.7 us
    all_gather x1 -> x0, waiting for transfers between devices: 28.3 us -> none  [body(): slot_block = lax.all_gather(slot_block, 'core', axis=0, tiled=True)]
    all_to_all x0 -> x1, blocking collectives: none -> 18.1 us  [body(): lax.all_to_all(jnp.stack([slot_block] * lax.axis_size('core')), 'core', 0...]
    dot_general x1, matrix products: 13.3 us -> 7.71 us  [body(): up_pre = jnp.dot(slot_block, w_up[0], preferred_element_type=jnp.float32)]
    all_gather x1, waiting for transfers between devices: 39.9 us -> 34.8 us  [body(): lax.all_gather(own_keys, ('xh', 'core'), axis=1, tiled=True)]
  transfers between devices with their start and end apart: 2 -> 1, of which waited for: 2 -> 1; matrix products, arithmetic and copies ran while one was open for 0% -> 0% of each run, Pallas kernels for 0% -> 0%
where the time goes in v1:
time: 195 us
  blocking collectives  114 us (58%)
  waiting for transfers between devices  34.9 us (18%)
  matrix products  29.7 us (15%)
  between operations  14.1 us (7%)
  other arithmetic  2.19 us (1%)
    all_to_all x1, blocking collectives, body(): lax.all_to_all(slot_rows, ('expert', 'xh'), split_axis=0, concat_axis=0,...  96.2 us
    all_gather x1, waiting for transfers between devices, body(): lax.all_gather(own_keys, ('xh', 'core'), axis=1, tiled=True)  34.8 us
    all_to_all x1, blocking collectives, body(): lax.all_to_all(jnp.stack([slot_block] * lax.axis_size('core')), 'core', 0...  18.1 us
    dot_general x1, matrix products, body(): jnp.dot(slot_block, w_gate[0], preferred_element_type=jnp.float32)  10.8 us
    dot_general x1, matrix products, body(): up_pre = jnp.dot(slot_block, w_up[0], preferred_element_type=jnp.float32)  7.71 us
    dot_general x1, matrix products, body(): jnp.einsum('rf,rg->fg', own_keys, lax.all_gather(own_keys, ('xh', 'core')...  6.9 us
    dot_general x1, matrix products, body(): jnp.dot(onehot.astype(tokens.dtype), tokens, preferred_element_type=jnp.f...  4.11 us
  transfers between devices with their start and end apart: 1, of which 1 were waited for; matrix products, arithmetic and copies ran while one was open for 0% of the time, Pallas kernels for 0%

profile of v1, /device:TPU:1, one launch (start us, length us, event | category | flops | bytes accessed | tf_op | source)
XLA Modules:
  0.0 195.2 jit_solution(7288430127100237932)
XLA Ops:
  6.5 0.0 all-gather.2.cloned.1.call-start
  7.2 0.7 fusion.7
  8.0 0.2 convolution_convert_fusion.1
  8.1 0.1 fusion.8
  8.3 4.1 %fusion = bf16[64,8,7168]{2,1,0:T(8,128)(2,1)S(1)} fusion(pred[512,256]{1,0:T(8,128)(4,1)S(1)} %bitcast.28, bf16[256,7168]{1,0:T(8,128)(2,1)} %param.5), kind=kOutput, calls=%fused_computation.2 | convolution fusion | flops 1882718208 | bytes 11141120 | tf_op jit(solution)/shard_map/dot_general | solution.py:34
  12.4 96.2 %all_to_all.10 = bf16[64,8,7168]{2,1,0:T(8,128)(2,1)S(1)} all-to-all(bf16[64,8,7168]{2,1,0:T(8,128)(2,1)S(1)} %fusion), channel_id=1, replica_groups=mesh['expert'=32,'xh'=2,'core'=2] {'expert','xh'}, dimensions={0} | all-to-all | bytes 14680064 | tf_op jit(solution)/shard_map/all_to_all | solution.py:38
  108.6 0.0 slice-start
  108.6 1.4 pad_maximum_fusion
  109.9 0.0 slice-start.1
  110.0 18.1 %all_to_all.11 = bf16[2,512,7168]{2,1,0:T(8,128)(2,1)S(1)} all-to-all(bf16[2,512,7168]{2,1,0:T(8,128)(2,1)S(1)} %pad_maximum_fusion), channel_id=1, replica_groups=mesh['expert'=32,'xh'=2,'core'=2] {'core'}, dimensions={0} | all-to-all | bytes 29360128 | tf_op jit(solution)/shard_map/all_to_all | solution.py:43
  128.0 0.0 slice-done
  128.0 0.0 slice-done.1
  128.0 7.7 %fusion.1 = f32[1024,512]{1,0:T(8,128)S(1)} fusion(bf16[1024,7168]{1,0:T(8,128)(2,1)S(1)} %bitcast.26, bf16[1,7168,512]{2,1,0:T(8,128)(2,1)S(1)} %bitcast.30), kind=kOutput, calls=%fused_computation.3 | convolution fusion | flops 7516192768 | bytes 24117248 | tf_op jit(solution)/shard_map/dot_general | solution.py:46
  135.7 10.8 %multiply_convert_fusion = bf16[1024,512]{1,0:T(8,128)(2,1)} fusion(f32[1024,512]{1,0:T(8,128)S(1)} %fusion.1, bf16[1024,7168]{1,0:T(8,128)(2,1)S(1)} %bitcast.27, bf16[1,7168,512]{2,1,0:T(8,128)(2,1)} %param.8), kind=kOutput, calls=%fused_computation.8 | convolution fusion | flops 7519338496 | bytes 25165824 | tf_op jit(solution)/shard_map/dot_general | solution.py:45
  146.6 0.0 all-gather.2.cloned.1.call-update
  146.6 34.8 %all-gather.2.cloned.1.call-done = bf16[1024,2048]{1,0:T(8,128)(2,1)} async-done(((bf16[1024,512]{1,0:T(8,128)(2,1)}), bf16[1024,2048]{1,0:T(8,128)(2,1)}) %all-gather.2.cloned.1.call-update) | async-done | bytes 4194320 | tf_op jit(solution)/shard_map/all_gather | solution.py:53
  181.5 6.9 %multiply_bitcast_fusion = f32[1,512,2048]{2,1,0:T(8,128)} fusion(bf16[1024,512]{1,0:T(8,128)(2,1)} %multiply_convert_fusion, bf16[1024,2048]{1,0:T(8,128)(2,1)} %all-gather.2.cloned.1.call-done), kind=kOutput, calls=%fused_computation.7 | convolution fusion | flops 2148532224 | bytes 9437184 | tf_op jit(solution)/shard_map/rf,rg->fg/dot_general | solution.py:50
  (4 shorter events, 0.1 us)
Async XLA Ops:
  6.5 174.9 %all-gather.2.cloned.1.call-start = ((), (), s32[]{:S(2)}) async-start(), calls=%async_computation.2 | async-start | bytes 5242880 | tf_op jit(solution)/shard_map/all_gather | solution.py:53
  108.6 19.5 %slice-start = ((s8[7340032]{0:T(1024)(128)(4,1)}), s8[4194304]{0:T(1024)(128)(4,1)S(1)}, s32[]{:S(2)}) async-start(s8[7340032]{0:T(1024)(128)(4,1)} %bitcast.29), calls=%async_computation.3 | async-start | bytes 8388608
  109.9 18.1 %slice-start.1 = ((s8[7340032]{0:T(1024)(128)(4,1)}), s8[3145728]{0:T(1024)(128)(4,1)S(1)}, s32[]{:S(2)}) async-start(s8[7340032]{0:T(1024)(128)(4,1)} %bitcast.29), calls=%async_computation.4 | async-start | bytes 6291456
Sparse Core Ops, SparseCore 0:
  146.7 34.6 all-gather.1
